TPU v7x, 256 devices: a whole 4x4x8 slice. The times are simulated.
256 devices in a mesh: tm: 32 (over y, x, core), tensor: 8 (over z).
Axes of the slice: x: 4, y: 4, z: 8, core: 2. Of those that a mesh axis runs over, the one named last changes fastest.
Arguments:
- features: bfloat16 [32768, 1536], P(('tm', 'tensor')), may hold values from -4 to 4
- frame_mask: int32 [32768], P('tm'), may hold values 0 or 1
- total_length: int32 [1], replicated, may hold values from 24576 to 32768
- norm_gain: float32 [1536], replicated, may hold values from 0.1 to 1.9
- value_weight: bfloat16 [1536, 1536], P(None, 'tensor'), may hold values from -0.15625 to 0.15625
- gate_weight: bfloat16 [1536, 1536], P(None, 'tensor'), may hold values from -0.15625 to 0.15625
- depth_kernel: float32 [31, 1536], P(None, 'tensor'), may hold values from -1 to 1
- batch_gain: float32 [1536], P('tensor'), may hold values from 0.1 to 1.9
- batch_bias: float32 [1536], P('tensor'), may hold values from -2 to 2
- out_weight: bfloat16 [1536, 1536], P('tensor'), may hold values from -0.15625 to 0.15625
- feed_gain: float32 [1536], replicated, may hold values from 0.1 to 1.9
- up_weight: bfloat16 [1536, 6144], P('tm', 'tensor'), may hold values from -0.15625 to 0.15625
- down_weight: bfloat16 [6144, 1536], P('tensor', 'tm'), may hold values from -0.078125 to 0.078125
Outputs:
- encoded: bfloat16 [32768, 1536], P(('tm', 'tensor'))
All inputs are finite; a program needn't handle non-finite values. No bound on the sum of `frame_mask` on one device may be relied on, other than what follows from the above.
Results may differ from a plain program's by a relative error of at most 0.0074.
Values may be sent and summed in bfloat16 or wider, within the bound.
No kernel may reach another device: no remote copies, remote signals or barrier semaphores. Data moves between devices by JAX's collectives and lax.ppermute only.
A program may use at most 64 MiB of HBM per device.

v0:
```python
import jax
import jax.numpy as jnp
from jax import lax
from jax.sharding import PartitionSpec as P

KERNEL = 31


def extended(array, sides, width):
    for axis, dim in sides:
        devices, length = (lax.axis_size(axis), array.shape[dim])
        up = [(i, (i + 1) % devices) for i in range(devices - 1)]
        down = [(j, i) for i, j in up]
        last = lax.slice_in_dim(array, length - width, length, axis=dim)
        initial = lax.slice_in_dim(array, 0, width, axis=dim)
        before = lax.ppermute(last, axis, up)
        after = lax.ppermute(initial, axis, down)
        array = jnp.concatenate([before, array, after], axis=dim)
    return array


def layer_norm(rows, gain):
    values = rows.astype(jnp.float32)
    centre = jnp.mean(values, axis=-1, keepdims=True)
    spread = jnp.mean(jnp.square(values - centre), axis=-1, keepdims=True)
    return (values - centre) * lax.rsqrt(spread + 1e-05) * gain


def merge_moments(low, high):
    n_a, mean_a, m2_a = (low[0], low[1], low[2])
    n_b, mean_b, m2_b = (high[0], high[1], high[2])
    n = n_a + n_b
    share = jnp.where(n > 0, n_b / jnp.maximum(n, 1.0), 0.0)
    delta = mean_b - mean_a
    mean = mean_a + delta * share
    m2 = m2_a + m2_b + jnp.square(delta) * n_a * share
    return jnp.stack([n, mean, m2])


def moments_over(stats, axis):
    size = lax.axis_size(axis)
    me = lax.axis_index(axis)
    step = 1
    while step < size:
        pairs = [(i, i ^ step) for i in range(size)]
        other = lax.ppermute(stats, axis, pairs)
        mine_low = me & step == 0
        low = jnp.where(mine_low, stats, other)
        high = jnp.where(mine_low, other, stats)
        stats = merge_moments(low, high)
        step *= 2
    return stats


def shards(
    features,
    frame_mask,
    total_length,
    norm_gain,
    value_weight,
    gate_weight,
    depth_kernel,
    batch_gain,
    batch_bias,
    out_weight,
    feed_gain,
    up_weight,
    down_weight,
):
    own_rows = features.shape[0]
    block = own_rows * lax.axis_size("tensor")
    positions = lax.axis_index("tm") * block + jnp.arange(block, dtype=jnp.int32)
    valid = ((frame_mask > 0) & (positions < total_length[0])).astype(jnp.float32)
    normed = layer_norm(features, norm_gain).astype(jnp.bfloat16)
    piece = lax.all_gather(normed, "tensor", axis=0, tiled=True)
    up_whole = lax.all_gather(up_weight, "tm", axis=0, tiled=True)
    down_whole = lax.all_gather(down_weight, "tm", axis=1, tiled=True)
    value = jnp.dot(piece, value_weight, preferred_element_type=jnp.float32)
    gate = jnp.dot(piece, gate_weight, preferred_element_type=jnp.float32)
    glu = (value * jax.nn.sigmoid(gate) * valid[:, None]).astype(jnp.bfloat16)
    padded = extended(glu, (("tm", 0),), KERNEL // 2)
    conv = jnp.zeros(glu.shape, jnp.float32)
    for tap in range(KERNEL):
        conv = conv + padded[tap : tap + block].astype(jnp.float32) * depth_kernel[tap]
    count_local = jnp.sum(valid)
    local_sum = jnp.sum(conv * valid[:, None], axis=0)
    local_mean = jnp.where(count_local > 0, local_sum / jnp.maximum(count_local, 1.0), 0.0)
    local_m2 = jnp.sum(jnp.square(conv - local_mean) * valid[:, None], axis=0)
    stats = jnp.stack([jnp.broadcast_to(count_local, local_sum.shape), local_mean, local_m2])
    stats = moments_over(stats, "tm")
    count, mean, m2 = (stats[0], stats[1], stats[2])
    centred = conv - mean
    var = m2 / count
    scaled = centred * lax.rsqrt(var + 1e-05) * batch_gain + batch_bias
    swished = (scaled * jax.nn.sigmoid(scaled)).astype(jnp.bfloat16)
    conv_part = jnp.dot(swished, out_weight, preferred_element_type=jnp.float32)
    conv_part, up_whole, down_whole = lax.optimization_barrier((conv_part, up_whole, down_whole))
    conv_out = lax.psum_scatter(
        conv_part.astype(jnp.bfloat16), "tensor", scatter_dimension=0, tiled=True
    ).astype(jnp.float32)
    mid = (features.astype(jnp.float32) + conv_out).astype(jnp.bfloat16)
    feed_normed = layer_norm(mid, feed_gain).astype(jnp.bfloat16)
    feed_block = lax.all_gather(feed_normed, "tensor", axis=0, tiled=True)
    pre = jnp.dot(feed_block, up_whole, preferred_element_type=jnp.float32)
    hidden = (pre * jax.nn.sigmoid(pre)).astype(jnp.bfloat16)
    partial_out = jnp.dot(hidden, down_whole, preferred_element_type=jnp.float32)
    feed_out = lax.psum_scatter(
        partial_out.astype(jnp.bfloat16), "tensor", scatter_dimension=0, tiled=True
    ).astype(jnp.float32)
    return (mid.astype(jnp.float32) + 0.5 * feed_out).astype(jnp.bfloat16)


def solution(mesh):
    placed = (
        P(("tm", "tensor"), None),
        P("tm"),
        P(),
        P(),
        P(None, "tensor"),
        P(None, "tensor"),
        P(None, "tensor"),
        P("tensor"),
        P("tensor"),
        P("tensor", None),
        P(),
        P("tm", "tensor"),
        P("tensor", "tm"),
    )
    return jax.shard_map(
        shards, mesh=mesh, in_specs=placed, out_specs=P(("tm", "tensor"), None), check_vma=False
    )
```

profile of v0, /device:TPU:2, one launch (start us, length us, event | category | flops | bytes accessed | tf_op | source)
XLA Modules:
  0.0 321.7 jit_solution(17575117318898476684)
XLA Ops:
  6.5 1.2 convert_reduce_fusion.1
  7.7 1.2 fusion.13
  9.0 2.0 fusion.15
  11.1 0.7 all-gather.7.cloned.1.call-update
  11.8 0.7 all-gather.9.cloned.1.call-update
  13.2 1.0 fusion.66
  14.3 1.4 fusion.63
  15.6 43.5 %all-gather.5.cloned.1.call-done = bf16[1024,1536]{1,0:T(8,128)(2,1)} async-done(((bf16[128,1536]{1,0:T(8,128)(2,1)}), bf16[1024,1536]{1,0:T(8,128)(2,1)}) %all-gather.5.cloned.1.call-update) | async-done | bytes 3145744 | tf_op jit(solution)/shard_map/all_gather | solution.py:75
  59.1 3.4 %fusion.4 = f32[1024,192]{0,1:T(8,128)S(1)} fusion(bf16[1024,1536]{1,0:T(8,128)(2,1)} %all-gather.5.cloned.1.call-done, bf16[1536,192]{0,1:T(8,128)(2,1)} %param.18), kind=kOutput, calls=%fused_computation.36 | convolution fusion | flops 604569600 | bytes 4521984 | tf_op jit(solution)/shard_map/dot_general | solution.py:79
  62.6 1.2 fusion.5
  63.9 1.9 collective-permute-start
  65.8 3.6 %collective-permute-start.1 = (bf16[15,192]{0,1:T(8,128)(2,1)S(1)}, bf16[15,192]{0,1:T(8,128)(2,1)S(1)}, u32[]{:S(2)}, u32[]{:S(2)}) collective-permute-start(bf16[15,192]{0,1:T(8,128)(2,1)S(1)} %get-tuple-element.32), channel_id=1, source_target_pairs={{8,0},{16,8},{24,16},{32,24},{40,32},{48,40},{56,48},{64,56},{72,6... | collective-permute-start | bytes 17288 | tf_op jit(solution)/shard_map/ppermute | solution.py:17
  69.4 1.0 fusion.67
  72.4 5.6 %multiply_reduce_fusion.1 = (f32[192]{0:T(256)S(1)}, f32[1024,192]{0,1:T(8,128)S(1)}) fusion(f32[1024]{0:T(1024)S(1)} %get-tuple-element.28, f32[192]{0:T(256)S(1)} %bitcast.79, bf16[15,192]{0,1:T(8,128)(2,1)S(1)} %collective-permute-done.1, bf16[1024,192]{0,1:T(8,128)(2,1)S(1)} %fusion.5, f32[192]{0:T(256)S(1)} %bitcast.80, f32[192]{0:T(256)S(1)} %bitcast.51, ...), kind=kLoop, calls=%fused_computation.58 | loop fusion | flops 36175680 | bytes 1219840 | tf_op jit(solution)/shard_map/reduce_sum | solution.py:86
  78.7 0.8 collective-permute-done.2
  80.3 3.1 collective-permute-done.3
  83.5 4.3 %collective-permute-start.4 = (f32[3,192]{1,0:T(4,128)S(1)}, f32[3,192]{1,0:T(4,128)S(1)}, u32[]{:S(2)}, u32[]{:S(2)}) collective-permute-start(f32[3,192]{1,0:T(4,128)S(1)} %pad_maximum_fusion.4), channel_id=1, source_target_pairs={{0,32},{8,40},{16,48},{24,56},{32,0},{40,8},{48,16},{56,24},{64,96... | collective-permute-start | bytes 6920 | tf_op jit(solution)/shard_map/ppermute | solution.py:46
  87.7 1.6 collective-permute-done.4
  89.4 1.6 collective-permute-start.5
  91.0 2.1 collective-permute-done.5
  93.2 3.2 collective-permute-start.6
  96.4 2.3 collective-permute-done.6
  98.7 2.9 fusion.18
  101.6 7.7 %all-gather.7.cloned.1.call-done = bf16[1536,768]{1,0:T(8,128)(2,1)} async-done(((bf16[48,768]{1,0:T(8,128)(2,1)}), bf16[1536,768]{1,0:T(8,128)(2,1)}) %all-gather.7.cloned.1.call-update) | async-done | bytes 2359312 | tf_op jit(solution)/shard_map/all_gather | solution.py:76
  109.3 51.2 %all-gather.9.cloned.1.call-done = bf16[768,1536]{0,1:T(8,128)(2,1)} async-done(((bf16[768,48]{0,1:T(8,128)(2,1)}), bf16[768,1536]{0,1:T(8,128)(2,1)}) %all-gather.9.cloned.1.call-update) | async-done | bytes 2359312 | tf_op jit(solution)/shard_map/all_gather | solution.py:77
  160.6 48.8 %reduce-scatter.3.cloned.1.call-done = bf16[128,1536]{1,0:T(8,128)(2,1)} async-done(((bf16[1024,1536]{1,0:T(8,128)(2,1)}), bf16[128,1536]{1,0:T(8,128)(2,1)}) %reduce-scatter.3.cloned.1.call-update) | async-done | bytes 393232 | tf_op jit(solution)/shard_map/reduce_scatter | solution.py:98
  209.3 1.2 convert_reduce_fusion
  210.8 1.0 fusion.12
  211.9 44.4 %all-gather.11.cloned.1.call-done = bf16[1024,1536]{1,0:T(8,128)(2,1)} async-done(((bf16[128,1536]{1,0:T(8,128)(2,1)}), bf16[1024,1536]{1,0:T(8,128)(2,1)}) %all-gather.11.cloned.1.call-update) | async-done | bytes 3145744 | tf_op jit(solution)/shard_map/all_gather | solution.py:103
  256.4 11.1 %convolution_convert_fusion = bf16[1024,1536]{1,0:T(8,128)(2,1)} fusion(bf16[768,1536]{0,1:T(8,128)(2,1)} %all-gather.9.cloned.1.call-done, bf16[1024,1536]{1,0:T(8,128)(2,1)} %all-gather.11.cloned.1.call-done, bf16[1536,768]{1,0:T(8,128)(2,1)} %all-gather.7.cloned.1.call-done), kind=kOutput, calls=%fused_computation | convolution fusion | flops 4837343232 | bytes 11010048 | tf_op jit(solution)/shard_map/dot_general | solution.py:106
  267.4 45.6 %reduce-scatter.5.cloned.1.call-done = bf16[128,1536]{1,0:T(8,128)(2,1)} async-done(((bf16[1024,1536]{1,0:T(8,128)(2,1)}), bf16[128,1536]{1,0:T(8,128)(2,1)}) %reduce-scatter.5.cloned.1.call-update) | async-done | bytes 393232 | tf_op jit(solution)/shard_map/reduce_scatter | solution.py:107
  313.0 1.9 fusion.17
  (57 shorter events, 3.0 us)
Async XLA Ops:
  6.5 92.2 %copy-start = (bf16[192,1536]{1,0:T(8,128)(2,1)S(1)}, bf16[192,1536]{1,0:T(8,128)(2,1)}, u32[]{:S(2)}) copy-start(bf16[192,1536]{1,0:T(8,128)(2,1)} %param.22) | copy-start | bytes 1769476
  6.5 52.6 %all-gather.5.cloned.1.call-start = ((), (), s32[]{:S(2)}) async-start(), calls=%async_computation.2 | async-start | bytes 3538944 | tf_op jit(solution)/shard_map/all_gather | solution.py:75
  11.1 98.3 %all-gather.7.cloned.1.call-start = ((), (), s32[]{:S(2)}) async-start(), calls=%async_computation.3 | async-start | bytes 2433024 | tf_op jit(solution)/shard_map/all_gather | solution.py:76
  11.8 148.7 %all-gather.9.cloned.1.call-start = ((), (), s32[]{:S(2)}) async-start(), calls=%async_computation.4 | async-start | bytes 2433024 | tf_op jit(solution)/shard_map/all_gather | solution.py:77
  12.5 196.8 %reduce-scatter.3.cloned.1.call-start = ((), (), s32[]{:S(2)}) async-start(), calls=%async_computation.5 | async-start | bytes 3538944 | tf_op jit(solution)/shard_map/reduce_scatter | solution.py:98
  15.6 46.9 %copy-start.4 = (bf16[1536,192]{0,1:T(8,128)(2,1)S(1)}, bf16[1536,192]{0,1:T(8,128)(2,1)}, u32[]{:S(2)}) copy-start(bf16[1536,192]{0,1:T(8,128)(2,1)} %param.17) | copy-start | bytes 1769476
  59.1 3.4 %copy-start.3 = (bf16[1024,1536]{1,0:T(8,128)(2,1)S(1)}, bf16[1024,1536]{1,0:T(8,128)(2,1)}, u32[]{:S(2)}) copy-start(bf16[1024,1536]{1,0:T(8,128)(2,1)} %all-gather.5.cloned.1.call-done) | copy-start | bytes 9437188
  62.6 36.1 %copy-start.5 = (f32[192]{0:T(256)S(1)}, f32[192]{0:T(256)}, u32[]{:S(2)}) copy-start(f32[192]{0:T(256)} %param.21) | copy-start | bytes 2308
  62.6 36.1 %copy-start.6 = (f32[192]{0:T(256)S(1)}, f32[192]{0:T(256)}, u32[]{:S(2)}) copy-start(f32[192]{0:T(256)} %param.20) | copy-start | bytes 2308
  63.9 8.5 %collective-permute-start = (bf16[15,192]{0,1:T(8,128)(2,1)S(1)}, bf16[15,192]{0,1:T(8,128)(2,1)S(1)}, u32[]{:S(2)}, u32[]{:S(2)}) collective-permute-start(bf16[15,192]{0,1:T(8,128)(2,1)S(1)} %get-tuple-element.31), channel_id=1, source_target_pairs={{0,8},{8,16},{16,24},{24,32},{32,40},{40,48},{48,56},{56,64},{64,7... | collective-permute-start | bytes 17288 | tf_op jit(solution)/shard_map/ppermute | solution.py:16
  65.8 6.6 %collective-permute-start.1 = (bf16[15,192]{0,1:T(8,128)(2,1)S(1)}, bf16[15,192]{0,1:T(8,128)(2,1)S(1)}, u32[]{:S(2)}, u32[]{:S(2)}) collective-permute-start(bf16[15,192]{0,1:T(8,128)(2,1)S(1)} %get-tuple-element.32), channel_id=1, source_target_pairs={{8,0},{16,8},{24,16},{32,24},{40,32},{48,40},{56,48},{64,56},{72,6... | collective-permute-start | bytes 17288 | tf_op jit(solution)/shard_map/ppermute | solution.py:17
  78.3 1.2 collective-permute-start.2
  79.7 3.7 %collective-permute-start.3 = (f32[3,192]{1,0:T(4,128)S(1)}, f32[3,192]{1,0:T(4,128)S(1)}, u32[]{:S(2)}, u32[]{:S(2)}) collective-permute-start(f32[3,192]{1,0:T(4,128)S(1)} %pad_maximum_fusion.3), channel_id=1, source_target_pairs={{0,16},{8,24},{16,0},{24,8},{32,48},{40,56},{48,32},{56,40},{64,80... | collective-permute-start | bytes 6920 | tf_op jit(solution)/shard_map/ppermute | solution.py:46
  83.5 5.9 %collective-permute-start.4 = (f32[3,192]{1,0:T(4,128)S(1)}, f32[3,192]{1,0:T(4,128)S(1)}, u32[]{:S(2)}, u32[]{:S(2)}) collective-permute-start(f32[3,192]{1,0:T(4,128)S(1)} %pad_maximum_fusion.4), channel_id=1, source_target_pairs={{0,32},{8,40},{16,48},{24,56},{32,0},{40,8},{48,16},{56,24},{64,96... | collective-permute-start | bytes 6920 | tf_op jit(solution)/shard_map/ppermute | solution.py:46
  89.4 3.7 %collective-permute-start.5 = (f32[3,192]{1,0:T(4,128)S(1)}, f32[3,192]{1,0:T(4,128)S(1)}, u32[]{:S(2)}, u32[]{:S(2)}) collective-permute-start(f32[3,192]{1,0:T(4,128)S(1)} %pad_maximum_fusion.5), channel_id=1, source_target_pairs={{0,64},{8,72},{16,80},{24,88},{32,96},{40,104},{48,112},{56,120},{... | collective-permute-start | bytes 6920 | tf_op jit(solution)/shard_map/ppermute | solution.py:46
  93.2 5.5 %collective-permute-start.6 = (f32[3,192]{1,0:T(4,128)S(1)}, f32[3,192]{1,0:T(4,128)S(1)}, u32[]{:S(2)}, u32[]{:S(2)}) collective-permute-start(f32[3,192]{1,0:T(4,128)S(1)} %pad_maximum_fusion.6), channel_id=1, source_target_pairs={{0,128},{8,136},{16,144},{24,152},{32,160},{40,168},{48,176},{56,1... | collective-permute-start | bytes 6920 | tf_op jit(solution)/shard_map/ppermute | solution.py:46
  101.6 107.8 %copy-start.1 = (bf16[128,1536]{1,0:T(8,128)(2,1)S(1)}, bf16[128,1536]{1,0:T(8,128)(2,1)}, u32[]{:S(2)}) copy-start(bf16[128,1536]{1,0:T(8,128)(2,1)} %param.13) | copy-start | bytes 1179652
  101.6 109.2 %copy-start.2 = (f32[1536]{0:T(1024)S(1)}, f32[1536]{0:T(1024)}, u32[]{:S(2)}) copy-start(f32[1536]{0:T(1024)} %param.23) | copy-start | bytes 18436
  160.5 95.9 %all-gather.11.cloned.1.call-start = ((), (), s32[]{:S(2)}) async-start(), calls=%async_computation.6 | async-start | bytes 3538944 | tf_op jit(solution)/shard_map/all_gather | solution.py:103
  211.9 101.1 %reduce-scatter.5.cloned.1.call-start = ((), (), s32[]{:S(2)}) async-start(), calls=%async_computation.7 | async-start | bytes 3538944 | tf_op jit(solution)/shard_map/reduce_scatter | solution.py:107
Sparse Core Ops, SparseCore 0:
  11.2 47.9 all-gather.4
  61.7 47.5 all-gather.6
  111.8 48.5 all-gather.8
  162.9 46.4 reduce-scatter.2
  212.0 44.3 all-gather.10
  267.6 45.4 reduce-scatter.4
where the time goes:
time: 322 us
  waiting for transfers between devices  253 us (79%)
  matrix products  18.5 us (6%)
  other arithmetic  16.4 us (5%)
  starting transfers between devices  15.9 us (5%)
  between operations  15.7 us (5%)
    all_gather x1, waiting for transfers between devices, shards(): down_whole = lax.all_gather(down_weight, 'tm', axis=1, tiled=True)  51.2 us
    reduce_scatter x1, waiting for transfers between devices, shards(): lax.psum_scatter(conv_part.astype(jnp.bfloat16), 'tensor', scatter_dimens...  48.8 us
    reduce_scatter x1, waiting for transfers between devices, shards(): lax.psum_scatter(partial_out.astype(jnp.bfloat16), 'tensor', scatter_dime...  45.6 us
    all_gather x1, waiting for transfers between devices, shards(): feed_block = lax.all_gather(feed_normed, 'tensor', axis=0, tiled=True)  44.4 us
    all_gather x1, waiting for transfers between devices, shards(): piece = lax.all_gather(normed, 'tensor', axis=0, tiled=True)  43.5 us
    dot_general x1, matrix products, shards(): jnp.dot(hidden, down_whole, preferred_element_type=jnp.float32)  11.1 us
    ppermute x5, starting transfers between devices, moments_over(): other = lax.ppermute(stats, axis, pairs)  10.1 us
    ppermute x5, waiting for transfers between devices, moments_over(): other = lax.ppermute(stats, axis, pairs)  9.85 us
  transfers between devices with their start and end apart: 13, of which 11 were waited for; matrix products, arithmetic and copies ran while one was open for 6% of the time, Pallas kernels for 0%

commit v1 on v0

--- a/solution.py
+++ b/solution.py
@@ -4,6 +4,15 @@
 from jax.sharding import PartitionSpec as P
 
 KERNEL = 31
+
+
+def answer_entries(local_values):
+    column = []
+    for _ in range(lax.psum(1, axis_name="tensor")):
+        column.append(local_values)
+    m_next = jnp.stack(column)
+    plain = lax.all_to_all(m_next, "tensor", split_axis=0, concat_axis=0)
+    return jnp.concatenate(plain, axis=0)
 
 
 def extended(array, sides, width):
@@ -100,7 +109,7 @@
     ).astype(jnp.float32)
     mid = (features.astype(jnp.float32) + conv_out).astype(jnp.bfloat16)
     feed_normed = layer_norm(mid, feed_gain).astype(jnp.bfloat16)
-    feed_block = lax.all_gather(feed_normed, "tensor", axis=0, tiled=True)
+    feed_block = answer_entries(feed_normed)
     pre = jnp.dot(feed_block, up_whole, preferred_element_type=jnp.float32)
     hidden = (pre * jax.nn.sigmoid(pre)).astype(jnp.bfloat16)
     partial_out = jnp.dot(hidden, down_whole, preferred_element_type=jnp.float32)

time: 322 us -> 350 us (1.087)
  blocking collectives: 0 us -> 76.4 us
  waiting for transfers between devices: 253 us -> 206 us
    all_to_all x0 -> x1, blocking collectives: none -> 76.4 us  [answer_entries(): plain = lax.all_to_all(m_next, 'tensor', split_axis=0, concat_axis=0)]
    all_gather x1 -> x0, waiting for transfers between devices: 44.4 us -> none  [shards(): feed_block = lax.all_gather(feed_normed, 'tensor', axis=0, tiled=True)]
  transfers between devices with their start and end apart: 13 -> 12, of which waited for: 11 -> 10; matrix products, arithmetic and copies ran while one was open for 6% -> 5% of each run, Pallas kernels for 0% -> 0%
where the time goes in v1:
time: 350 us; the launch traced here: 349 us
  waiting for transfers between devices  206 us (59%)
  blocking collectives  76.4 us (22%)
  matrix products  17.2 us (5%)
  starting transfers between devices  15.8 us (5%)
  other arithmetic  15.7 us (4%)
  between operations  15.3 us (4%)
    all_to_all x1, blocking collectives, answer_entries(): plain = lax.all_to_all(m_next, 'tensor', split_axis=0, concat_axis=0)  76.4 us
    all_gather x1, waiting for transfers between devices, shards(): down_whole = lax.all_gather(down_weight, 'tm', axis=1, tiled=True)  51.2 us
    reduce_scatter x1, waiting for transfers between devices, shards(): lax.psum_scatter(conv_part.astype(jnp.bfloat16), 'tensor', scatter_dimens...  48.8 us
    all_gather x1, waiting for transfers between devices, shards(): piece = lax.all_gather(normed, 'tensor', axis=0, tiled=True)  43.5 us
    reduce_scatter x1, waiting for transfers between devices, shards(): lax.psum_scatter(partial_out.astype(jnp.bfloat16), 'tensor', scatter_dime...  43 us
    ppermute x5, starting transfers between devices, moments_over(): other = lax.ppermute(stats, axis, pairs)  10.1 us
    ppermute x5, waiting for transfers between devices, moments_over(): other = lax.ppermute(stats, axis, pairs)  9.85 us
    dot_general x1, matrix products, shards(): jnp.dot(hidden, down_whole, preferred_element_type=jnp.float32)  9.81 us
  transfers between devices with their start and end apart: 12, of which 10 were waited for; matrix products, arithmetic and copies ran while one was open for 5% of the time, Pallas kernels for 0%

profile of v1, /device:TPU:2, one launch (start us, length us, event | category | flops | bytes accessed | tf_op | source)
XLA Modules:
  0.0 349.0 jit_solution(9176615563717747247)
XLA Ops:
  6.5 1.2 convert_reduce_fusion.1
  7.7 1.2 fusion.13
  9.0 2.0 fusion.15
  11.1 0.7 all-gather.6.cloned.1.call-update
  11.8 0.7 all-gather.8.cloned.1.call-update
  13.2 1.0 fusion.66
  14.3 1.4 fusion.63
  15.6 43.5 %all-gather.4.cloned.1.call-done = bf16[1024,1536]{1,0:T(8,128)(2,1)} async-done(((bf16[128,1536]{1,0:T(8,128)(2,1)}), bf16[1024,1536]{1,0:T(8,128)(2,1)}) %all-gather.4.cloned.1.call-update) | async-done | bytes 3145744 | tf_op jit(solution)/shard_map/all_gather | solution.py:84
  59.1 3.4 fusion.4
  62.6 1.2 fusion.5
  63.9 1.9 collective-permute-start
  65.8 3.6 %collective-permute-start.1 = (bf16[15,192]{0,1:T(8,128)(2,1)S(1)}, bf16[15,192]{0,1:T(8,128)(2,1)S(1)}, u32[]{:S(2)}, u32[]{:S(2)}) collective-permute-start(bf16[15,192]{0,1:T(8,128)(2,1)S(1)} %get-tuple-element.32), channel_id=1, source_target_pairs={{8,0},{16,8},{24,16},{32,24},{40,32},{48,40},{56,48},{64,56},{72,6... | collective-permute-start | bytes 17288 | tf_op jit(solution)/shard_map/ppermute | solution.py:26
  69.4 1.0 fusion.67
  72.4 5.6 %multiply_reduce_fusion.1 = (f32[192]{0:T(256)S(1)}, f32[1024,192]{0,1:T(8,128)S(1)}) fusion(f32[1024]{0:T(1024)S(1)} %get-tuple-element.28, f32[192]{0:T(256)S(1)} %bitcast.81, bf16[15,192]{0,1:T(8,128)(2,1)S(1)} %collective-permute-done.1, bf16[1024,192]{0,1:T(8,128)(2,1)S(1)} %fusion.5, f32[192]{0:T(256)S(1)} %bitcast.82, f32[192]{0:T(256)S(1)} %bitcast.53, ...), kind=kLoop, calls=%fused_computation.58 | loop fusion | flops 36175680 | bytes 1219840 | tf_op jit(solution)/shard_map/reduce_sum | solution.py:95
  78.7 0.8 collective-permute-done.2
  79.7 0.6 collective-permute-start.3
  80.3 3.1 collective-permute-done.3
  83.5 4.3 %collective-permute-start.4 = (f32[3,192]{1,0:T(4,128)S(1)}, f32[3,192]{1,0:T(4,128)S(1)}, u32[]{:S(2)}, u32[]{:S(2)}) collective-permute-start(f32[3,192]{1,0:T(4,128)S(1)} %pad_maximum_fusion.4), channel_id=1, source_target_pairs={{0,32},{8,40},{16,48},{24,56},{32,0},{40,8},{48,16},{56,24},{64,96... | collective-permute-start | bytes 6920 | tf_op jit(solution)/shard_map/ppermute | solution.py:55
  87.7 1.6 collective-permute-done.4
  89.4 1.6 collective-permute-start.5
  91.0 2.1 collective-permute-done.5
  93.2 3.2 collective-permute-start.6
  96.4 2.3 collective-permute-done.6
  98.7 2.9 fusion.18
  101.6 7.7 %all-gather.6.cloned.1.call-done = bf16[1536,768]{1,0:T(8,128)(2,1)} async-done(((bf16[48,768]{1,0:T(8,128)(2,1)}), bf16[1536,768]{1,0:T(8,128)(2,1)}) %all-gather.6.cloned.1.call-update) | async-done | bytes 2359312 | tf_op jit(solution)/shard_map/all_gather | solution.py:85
  109.3 51.2 %all-gather.8.cloned.1.call-done = bf16[768,1536]{0,1:T(8,128)(2,1)} async-done(((bf16[768,48]{0,1:T(8,128)(2,1)}), bf16[768,1536]{0,1:T(8,128)(2,1)}) %all-gather.8.cloned.1.call-update) | async-done | bytes 2359312 | tf_op jit(solution)/shard_map/all_gather | solution.py:86
  160.6 48.8 %reduce-scatter.3.cloned.1.call-done = bf16[128,1536]{1,0:T(8,128)(2,1)} async-done(((bf16[1024,1536]{1,0:T(8,128)(2,1)}), bf16[128,1536]{1,0:T(8,128)(2,1)}) %reduce-scatter.3.cloned.1.call-update) | async-done | bytes 393232 | tf_op jit(solution)/shard_map/reduce_scatter | solution.py:107
  209.3 1.2 convert_reduce_fusion
  211.4 76.4 %all_to_all.5 = bf16[8,128,1536]{2,1,0:T(8,128)(2,1)} all-to-all(bf16[8,128,1536]{2,1,0:T(8,128)(2,1)S(1)} %stack.20), channel_id=1, replica_groups=mesh['tm'=32,'tensor'=8] {'tensor'}, dimensions={0} | all-to-all | bytes 6291456 | tf_op jit(solution)/shard_map/all_to_all | solution.py:14
  287.8 9.8 %convolution_convert_fusion = bf16[1024,1536]{1,0:T(8,128)(2,1)} fusion(bf16[768,1536]{0,1:T(8,128)(2,1)} %all-gather.8.cloned.1.call-done, bf16[1024,1536]{1,0:T(8,128)(2,1)} %bitcast.47, bf16[1536,768]{1,0:T(8,128)(2,1)S(1)} %copy-done.4), kind=kOutput, calls=%fused_computation | convolution fusion | flops 4837343232 | bytes 11010048 | tf_op jit(solution)/shard_map/dot_general | solution.py:115
  297.6 43.0 %reduce-scatter.5.cloned.1.call-done = bf16[128,1536]{1,0:T(8,128)(2,1)} async-done(((bf16[1024,1536]{1,0:T(8,128)(2,1)}), bf16[128,1536]{1,0:T(8,128)(2,1)}) %reduce-scatter.5.cloned.1.call-update) | async-done | bytes 393232 | tf_op jit(solution)/shard_map/reduce_scatter | solution.py:116
  340.7 1.9 fusion.17
  (58 shorter events, 2.8 us)
Async XLA Ops:
  6.5 92.2 %copy-start = (bf16[192,1536]{1,0:T(8,128)(2,1)S(1)}, bf16[192,1536]{1,0:T(8,128)(2,1)}, u32[]{:S(2)}) copy-start(bf16[192,1536]{1,0:T(8,128)(2,1)} %param.22) | copy-start | bytes 1769476
  6.5 52.6 %all-gather.4.cloned.1.call-start = ((), (), s32[]{:S(2)}) async-start(), calls=%async_computation.3 | async-start | bytes 3538944 | tf_op jit(solution)/shard_map/all_gather | solution.py:84
  11.1 98.3 %all-gather.6.cloned.1.call-start = ((), (), s32[]{:S(2)}) async-start(), calls=%async_computation.4 | async-start | bytes 2433024 | tf_op jit(solution)/shard_map/all_gather | solution.py:85
  11.8 148.7 %all-gather.8.cloned.1.call-start = ((), (), s32[]{:S(2)}) async-start(), calls=%async_computation.5 | async-start | bytes 2433024 | tf_op jit(solution)/shard_map/all_gather | solution.py:86
  12.5 196.8 %reduce-scatter.3.cloned.1.call-start = ((), (), s32[]{:S(2)}) async-start(), calls=%async_computation.6 | async-start | bytes 3538944 | tf_op jit(solution)/shard_map/reduce_scatter | solution.py:107
  15.6 46.9 %copy-start.5 = (bf16[1536,192]{0,1:T(8,128)(2,1)S(1)}, bf16[1536,192]{0,1:T(8,128)(2,1)}, u32[]{:S(2)}) copy-start(bf16[1536,192]{0,1:T(8,128)(2,1)} %param.17) | copy-start | bytes 1769476
  59.1 3.4 copy-start.3
  62.6 36.1 %copy-start.6 = (f32[192]{0:T(256)S(1)}, f32[192]{0:T(256)}, u32[]{:S(2)}) copy-start(f32[192]{0:T(256)} %param.21) | copy-start | bytes 2308
  62.6 36.1 %copy-start.7 = (f32[192]{0:T(256)S(1)}, f32[192]{0:T(256)}, u32[]{:S(2)}) copy-start(f32[192]{0:T(256)} %param.20) | copy-start | bytes 2308
  63.9 8.5 %collective-permute-start = (bf16[15,192]{0,1:T(8,128)(2,1)S(1)}, bf16[15,192]{0,1:T(8,128)(2,1)S(1)}, u32[]{:S(2)}, u32[]{:S(2)}) collective-permute-start(bf16[15,192]{0,1:T(8,128)(2,1)S(1)} %get-tuple-element.31), channel_id=1, source_target_pairs={{0,8},{8,16},{16,24},{24,32},{32,40},{40,48},{48,56},{56,64},{64,7... | collective-permute-start | bytes 17288 | tf_op jit(solution)/shard_map/ppermute | solution.py:25
  65.8 6.6 %collective-permute-start.1 = (bf16[15,192]{0,1:T(8,128)(2,1)S(1)}, bf16[15,192]{0,1:T(8,128)(2,1)S(1)}, u32[]{:S(2)}, u32[]{:S(2)}) collective-permute-start(bf16[15,192]{0,1:T(8,128)(2,1)S(1)} %get-tuple-element.32), channel_id=1, source_target_pairs={{8,0},{16,8},{24,16},{32,24},{40,32},{48,40},{56,48},{64,56},{72,6... | collective-permute-start | bytes 17288 | tf_op jit(solution)/shard_map/ppermute | solution.py:26
  78.3 1.2 collective-permute-start.2
  79.7 3.7 %collective-permute-start.3 = (f32[3,192]{1,0:T(4,128)S(1)}, f32[3,192]{1,0:T(4,128)S(1)}, u32[]{:S(2)}, u32[]{:S(2)}) collective-permute-start(f32[3,192]{1,0:T(4,128)S(1)} %pad_maximum_fusion.3), channel_id=1, source_target_pairs={{0,16},{8,24},{16,0},{24,8},{32,48},{40,56},{48,32},{56,40},{64,80... | collective-permute-start | bytes 6920 | tf_op jit(solution)/shard_map/ppermute | solution.py:55
  83.5 5.9 %collective-permute-start.4 = (f32[3,192]{1,0:T(4,128)S(1)}, f32[3,192]{1,0:T(4,128)S(1)}, u32[]{:S(2)}, u32[]{:S(2)}) collective-permute-start(f32[3,192]{1,0:T(4,128)S(1)} %pad_maximum_fusion.4), channel_id=1, source_target_pairs={{0,32},{8,40},{16,48},{24,56},{32,0},{40,8},{48,16},{56,24},{64,96... | collective-permute-start | bytes 6920 | tf_op jit(solution)/shard_map/ppermute | solution.py:55
  89.4 3.7 %collective-permute-start.5 = (f32[3,192]{1,0:T(4,128)S(1)}, f32[3,192]{1,0:T(4,128)S(1)}, u32[]{:S(2)}, u32[]{:S(2)}) collective-permute-start(f32[3,192]{1,0:T(4,128)S(1)} %pad_maximum_fusion.5), channel_id=1, source_target_pairs={{0,64},{8,72},{16,80},{24,88},{32,96},{40,104},{48,112},{56,120},{... | collective-permute-start | bytes 6920 | tf_op jit(solution)/shard_map/ppermute | solution.py:55
  93.2 5.5 %collective-permute-start.6 = (f32[3,192]{1,0:T(4,128)S(1)}, f32[3,192]{1,0:T(4,128)S(1)}, u32[]{:S(2)}, u32[]{:S(2)}) collective-permute-start(f32[3,192]{1,0:T(4,128)S(1)} %pad_maximum_fusion.6), channel_id=1, source_target_pairs={{0,128},{8,136},{16,144},{24,152},{32,160},{40,168},{48,176},{56,1... | collective-permute-start | bytes 6920 | tf_op jit(solution)/shard_map/ppermute | solution.py:55
  101.6 107.8 %copy-start.1 = (bf16[128,1536]{1,0:T(8,128)(2,1)S(1)}, bf16[128,1536]{1,0:T(8,128)(2,1)}, u32[]{:S(2)}) copy-start(bf16[128,1536]{1,0:T(8,128)(2,1)} %param.13) | copy-start | bytes 1179652
  101.6 109.2 %copy-start.2 = (f32[1536]{0:T(1024)S(1)}, f32[1536]{0:T(1024)}, u32[]{:S(2)}) copy-start(f32[1536]{0:T(1024)} %param.23) | copy-start | bytes 18436
  160.5 180.1 %reduce-scatter.5.cloned.1.call-start = ((), (), s32[]{:S(2)}) async-start(), calls=%async_computation.7 | async-start | bytes 3538944 | tf_op jit(solution)/shard_map/reduce_scatter | solution.py:116
  211.4 76.4 %copy-start.4 = (bf16[1536,768]{1,0:T(8,128)(2,1)S(1)}, bf16[1536,768]{1,0:T(8,128)(2,1)}, u32[]{:S(2)}) copy-start(bf16[1536,768]{1,0:T(8,128)(2,1)} %all-gather.6.cloned.1.call-done) | copy-start | bytes 7077892
Sparse Core Ops, SparseCore 0:
  11.2 47.9 all-gather.3
  61.7 47.5 all-gather.5
  111.8 48.5 all-gather.7
  162.9 46.4 reduce-scatter.2
  297.7 42.8 reduce-scatter.4
